TPU v7x, 512 devices: a whole 4x8x8 slice. The times are simulated.
512 devices in a mesh: blk: 32 (over y, z_hi), kv: 16 (over z_lo, x, core).
Axes of the slice: x: 4, y: 8, z: 8 (z_hi: 4, z_lo: 2; z = z_hi * 2 + z_lo), core: 2. Of those that a mesh axis runs over, the one named last changes fastest.
Arguments:
- cache_entries: bfloat16 [65536, 8, 256], P(('kv', 'blk'))
- recompute_input: bfloat16 [4096, 4096], P('kv', 'blk'), may hold values from -6 to 6
- norm_gain: bfloat16 [4096], replicated, may hold values from 0.099609375 to 1.8984375
- w_query: bfloat16 [4096, 4096], P(None, 'blk'), may hold values from -0.25 to 0.25
- w_keyval: bfloat16 [4096, 2048], P('blk'), may hold values from -0.09375 to 0.09375
- w_out: bfloat16 [4096, 4096], P('blk'), may hold values from -0.09375 to 0.09375
- rotate_offsets: int32 [64], replicated, may hold values from 0 to 65535
- span_order: int32 [64], replicated, may hold values from 0 to 63, as said below
- tenant_of_span: int32 [64], replicated, may hold values from 0 to 3, never falling along the last dimension, each value on 1 to 32 neighbouring positions
- recompute_pos: int32 [4096], replicated, may hold values from 0 to 4095, as said below
- recompute_count: int32 [16], replicated, may hold values from 1 to 256, as said below
Outputs:
- attention_out: bfloat16 [4096, 4096], P('kv', 'blk')
Inputs may be any that keep to these rules, and one draw needn't show every extreme that they name: `span_order`: each aligned block of 4 entries is a permutation of the block slots of that same block. `tenant_of_span`: tenants never fall along the block slots; there are 4 tenants, one of exactly 32 blocks. `recompute_pos`: the 256 entries of each shard are distinct. `recompute_count`: at least one shard has all 256 slots live.
All inputs are finite; a program needn't handle non-finite values.
Results may differ from a plain program's by a relative error of at most 0.035.
Values may be sent and summed in bfloat16 or wider, within the bound.
No kernel may reach another device: no remote copies, remote signals or barrier semaphores. Data moves between devices by JAX's collectives and lax.ppermute only.
A program may use at most 64 MiB of HBM per device.

v0:
```python
import math
import jax
import jax.numpy as jnp
import numpy as np
from jax import lax
from jax.sharding import PartitionSpec as P

QH = 32
KVH = 8
HEAD_DIM = 128
WINDOW = 4096
SPAN = 1024
NEG_FILL = -1e30
ROPE_BASE = 10000.0
NORM_EPS = 1e-05


def shifted(shard, axis, by):
    devices = lax.axis_size(axis)
    pairs = [(i, i + by) for i in range(devices) if 0 <= i + by < devices]
    return lax.ppermute(shard, axis, pairs)


def rotate_half(values, positions):
    half = values.shape[-1] // 2
    inverse = ROPE_BASE ** (-(jnp.arange(half, dtype=jnp.float32) * 2.0 / values.shape[-1]))
    angles = positions.astype(jnp.float32)[:, None] * inverse[None, :]
    shape = (positions.shape[0],) + (1,) * (values.ndim - 2) + (half,)
    cosine = jnp.cos(angles).reshape(shape)
    sine = jnp.sin(angles).reshape(shape)
    first = values[..., :half]
    second = values[..., half:]
    return jnp.concatenate(
        [first * cosine - second * sine, second * cosine + first * sine], axis=-1
    )


def tenant_lookup(positions, tenant_of_span):
    span_ids = positions // SPAN
    table_index = jnp.arange(tenant_of_span.shape[0], dtype=jnp.int32)
    match = span_ids[:, None] == table_index[None, :]
    return jnp.sum(jnp.where(match, tenant_of_span[None, :], 0), axis=1)


def attend_part(queries, query_pos, query_tenant, keys, values, key_pos, key_tenant):
    scale = 1.0 / math.sqrt(keys.shape[-1])
    scores = jnp.einsum("cgh,sh->gcs", queries, keys, preferred_element_type=jnp.float32) * scale
    gap = query_pos[:, None] - key_pos[None, :]
    allowed = (
        (query_tenant[:, None] == key_tenant[None, :])
        & (gap >= 0)
        & (gap < WINDOW)
        & (key_pos[None, :] >= 0)
    )
    masked = jnp.where(allowed[None], scores, NEG_FILL)
    row_max = jnp.max(masked, axis=2)
    weights = jnp.where(allowed[None], jnp.exp(masked - row_max[..., None]), 0.0)
    totals = jnp.sum(weights, axis=2)
    summed = jnp.einsum(
        "gcs,sh->gch", weights.astype(jnp.bfloat16), values, preferred_element_type=jnp.float32
    )
    return (row_max, totals, summed)


def combine_parts(first, second):
    top = jnp.maximum(first[0], second[0])
    scale_one = jnp.exp(first[0] - top)
    scale_two = jnp.exp(second[0] - top)
    totals = first[1] * scale_one + second[1] * scale_two
    summed = first[2] * scale_one[..., None] + second[2] * scale_two[..., None]
    return summed / totals[..., None]


def local(
    cache_entries,
    recompute_input,
    norm_gain,
    w_query,
    w_keyval,
    w_out,
    rotate_offsets,
    span_order,
    tenant_of_span,
    recompute_pos,
    recompute_count,
):
    blk_count = lax.axis_size("blk")
    kv_index = lax.axis_index("kv")
    blk_index = lax.axis_index("blk")
    block_rows = cache_entries.shape[0]
    shard_len = block_rows * blk_count
    slots = recompute_input.shape[0]
    own_cols = recompute_input.shape[1]
    width = norm_gain.shape[0]
    local_heads = w_query.shape[1] // HEAD_DIM
    spans_here = shard_len // SPAN
    own_group = blk_index * local_heads // (QH // KVH)
    targets = np.arange(blk_count) * local_heads // (QH // KVH)
    wide = lax.all_gather(recompute_input, "blk", axis=1, tiled=True).astype(jnp.float32)
    gains = norm_gain.astype(jnp.float32)
    scaled = (wide * gains[None, :]).astype(jnp.bfloat16)
    query_acc = jnp.dot(scaled, w_query, preferred_element_type=jnp.float32)
    square_acc = jnp.sum(wide * wide, axis=1)
    own_gain = lax.dynamic_slice_in_dim(norm_gain, blk_index * own_cols, own_cols, 0).astype(
        jnp.float32
    )
    own_scaled = (recompute_input.astype(jnp.float32) * own_gain[None, :]).astype(jnp.bfloat16)
    pair_term = jnp.dot(own_scaled, w_keyval, preferred_element_type=jnp.float32)
    pair_sum = lax.psum(pair_term.astype(jnp.bfloat16), "blk").astype(jnp.float32)
    inv_rms = lax.rsqrt(square_acc / width + NORM_EPS)
    pair_heads = (pair_sum * inv_rms[:, None]).reshape(slots, KVH, 2 * HEAD_DIM)
    own_pair = lax.dynamic_index_in_dim(pair_heads, own_group, 1, keepdims=False)
    own_pos = lax.dynamic_slice_in_dim(recompute_pos, kv_index * slots, slots, 0)
    own_count = lax.dynamic_index_in_dim(recompute_count, kv_index, 0, keepdims=False)
    live = jnp.arange(slots, dtype=jnp.int32) < own_count
    query_pos = kv_index * shard_len + own_pos
    fresh_keys = rotate_half(own_pair[:, :HEAD_DIM], query_pos).astype(jnp.bfloat16)
    fresh_values = own_pair[:, HEAD_DIM:].astype(jnp.bfloat16)
    queries = rotate_half(
        (query_acc * inv_rms[:, None]).reshape(slots, local_heads, HEAD_DIM), query_pos
    ).astype(jnp.bfloat16)
    arrived = lax.all_to_all(
        jnp.take(cache_entries, targets, axis=1), "blk", split_axis=1, concat_axis=0, tiled=True
    )
    stored = arrived.reshape(shard_len, 2 * HEAD_DIM)
    offsets_here = lax.dynamic_slice_in_dim(rotate_offsets, kv_index * spans_here, spans_here, 0)
    row_shifts = jnp.repeat(offsets_here, SPAN, total_repeat_length=shard_len)
    turned_rows = rotate_half(stored[:, :HEAD_DIM].astype(jnp.float32), row_shifts).astype(
        jnp.bfloat16
    )
    stored = jnp.concatenate([turned_rows, stored[:, HEAD_DIM:]], axis=-1)
    local_order = (
        lax.dynamic_slice_in_dim(span_order, kv_index * spans_here, spans_here, 0)
        - kv_index * spans_here
    )
    ordered = jnp.take(stored.reshape(spans_here, SPAN, 2 * HEAD_DIM), local_order, axis=0).reshape(
        shard_len, 2 * HEAD_DIM
    )
    place = jnp.where(live, own_pos, shard_len)
    merged = ordered.at[place].set(jnp.concatenate([fresh_keys, fresh_values], axis=1), mode="drop")
    key_pos = kv_index * shard_len + jnp.arange(shard_len, dtype=jnp.int32)
    key_tenant = tenant_lookup(key_pos, tenant_of_span)
    query_tenant = tenant_lookup(query_pos, tenant_of_span)
    own_part = attend_part(
        queries,
        query_pos,
        query_tenant,
        merged[:, :HEAD_DIM],
        merged[:, HEAD_DIM:],
        key_pos,
        key_tenant,
    )
    prior = shifted(merged, "kv", 1)
    prior_pos = key_pos - shard_len
    prior_part = attend_part(
        queries,
        query_pos,
        query_tenant,
        prior[:, :HEAD_DIM],
        prior[:, HEAD_DIM:],
        prior_pos,
        tenant_lookup(prior_pos, tenant_of_span),
    )
    heads_out = combine_parts(own_part, prior_part).astype(jnp.bfloat16)
    out_rows = w_out.reshape(local_heads, HEAD_DIM, width)
    term = jnp.einsum("gch,ghd->cd", heads_out, out_rows, preferred_element_type=jnp.float32)
    summed_out = lax.psum_scatter(
        term.astype(jnp.bfloat16), "blk", scatter_dimension=1, tiled=True
    ).astype(jnp.float32)
    return jnp.where(live[:, None], summed_out, 0.0).astype(jnp.bfloat16)


def solution(mesh):
    placed = (
        P(("kv", "blk"), None, None),
        P("kv", "blk"),
        P(),
        P(None, "blk"),
        P("blk", None),
        P("blk", None),
        P(),
        P(),
        P(),
        P(),
        P(),
    )
    return jax.shard_map(
        local, mesh=mesh, in_specs=placed, out_specs=P("kv", "blk"), check_vma=False
    )
```

profile of v0, /device:TPU:2, one launch (start us, length us, event | category | flops | bytes accessed | tf_op | source)
XLA Modules:
  0.0 771.2 jit_solution(2034141246028215434)
XLA Ops:
  7.9 6.6 gather_fusion
  14.5 2.5 copy.21
  17.0 16.1 %all-to-all-start = ((bf16[128,32,256]{2,0,1:T(8,128)(2,1)}), bf16[128,32,256]{2,0,1:T(8,128)(2,1)S(1)}, u32[]{:S(2)}, u32[]{:S(2)}) async-start(bf16[128,32,256]{2,0,1:T(8,128)(2,1)} %copy.21), calls=%async_computation | async-start | bytes 4194304 | tf_op jit(solution)/shard_map/all_to_all | solution.py:122
  33.3 2.4 convolution_convert_fusion.1
  39.0 2.6 select_convert_fusion.1
  41.5 101.7 %all-gather.2.cloned.1.call-done = bf16[256,4096]{1,0:T(8,128)(2,1)} async-done(((bf16[256,128]{1,0:T(8,128)(2,1)}), bf16[256,4096]{1,0:T(8,128)(2,1)}) %all-gather.2.cloned.1.call-update) | async-done | bytes 2097168 | tf_op jit(solution)/shard_map/all_gather | solution.py:99
  143.3 2.1 fusion.4
  145.4 315.9 %all-reduce.2.cloned.1.call-done = bf16[256,2048]{1,0:T(8,128)(2,1)} async-done(((bf16[256,2048]{1,0:T(8,128)(2,1)}), bf16[256,2048]{1,0:T(8,128)(2,1)}) %all-reduce.2.cloned.1.call-update) | async-done | bytes 1048592 | tf_op jit(solution)/shard_map/psum | solution.py:109
  461.3 2.8 convert_multiply_fusion.2
  464.0 2.9 copy.27
  471.5 5.4 fusion.57
  478.9 3.5 pad_maximum_fusion
  482.4 2.3 gather_fusion.1
  484.7 1.9 bitcast_select_fusion
  486.6 4.8 scatter_fusion
  491.4 2.1 collective-permute-start
  494.1 2.7 fusion.36
  497.1 3.5 fusion.109
  500.6 18.3 %collective-permute-done = bf16[4096,256]{1,0:T(8,128)(2,1)S(1)} collective-permute-done((bf16[4096,256]{1,0:T(8,128)(2,1)}, bf16[4096,256]{1,0:T(8,128)(2,1)S(1)}, u32[]{:S(2)}, u32[]{:S(2)}) %collective-permute-start) | collective-permute-done | bytes 2097184 | tf_op jit(solution)/shard_map/ppermute | solution.py:21
  520.7 5.8 fusion.12
  526.5 3.0 fusion.39
  529.5 5.8 convolution_convert_fusion
  535.3 2.5 copy.28
  538.5 224.5 %reduce-scatter.4.cloned.1.call-done = bf16[128,256]{1,0:T(8,128)(2,1)} async-done(((bf16[4096,256]{1,0:T(8,128)(2,1)}), bf16[128,256]{1,0:T(8,128)(2,1)}) %reduce-scatter.4.cloned.1.call-update) | async-done | bytes 65552
  (68 shorter events, 16.3 us)
Async XLA Ops:
  6.5 523.0 %copy-start = (bf16[128,4096]{1,0:T(8,128)(2,1)S(1)}, bf16[128,4096]{1,0:T(8,128)(2,1)}, u32[]{:S(2)}) copy-start(bf16[128,4096]{1,0:T(8,128)(2,1)} %param.19) | copy-start | bytes 3145732
  6.5 136.7 %all-gather.2.cloned.1.call-start = ((), (), s32[]{:S(2)}) async-start(), calls=%async_computation.3 | async-start | bytes 2162688 | tf_op jit(solution)/shard_map/all_gather | solution.py:99
  14.5 18.7 %copy-start.4 = (bf16[4096]{0:T(1024)(128)(2,1)S(1)}, bf16[4096]{0:T(1024)(128)(2,1)}, u32[]{:S(2)}) copy-start(bf16[4096]{0:T(1024)(128)(2,1)} %param.16) | copy-start | bytes 24580
  14.5 18.8 %copy-start.3 = (bf16[256,128]{1,0:T(8,128)(2,1)S(1)}, bf16[256,128]{1,0:T(8,128)(2,1)}, u32[]{:S(2)}) copy-start(bf16[256,128]{1,0:T(8,128)(2,1)} %param.15) | copy-start | bytes 196612
  17.0 19.0 %copy-start.11 = (s32[16]{0:T(128)S(1)}, s32[16]{0:T(128)}, u32[]{:S(2)}) copy-start(s32[16]{0:T(128)} %param.24) | copy-start | bytes 196
  17.0 19.6 %copy-start.9 = (s32[64]{0:T(128)S(1)}, s32[64]{0:T(128)}, u32[]{:S(2)}) copy-start(s32[64]{0:T(128)} %param.21) | copy-start | bytes 772
  17.0 21.2 %copy-start.12 = (s32[64]{0:T(128)S(1)}, s32[64]{0:T(128)}, u32[]{:S(2)}) copy-start(s32[64]{0:T(128)} %param.20) | copy-start | bytes 772
  17.0 21.9 %copy-start.5 = (pred[4096]{0:T(1024)(128)(4,1)S(1)}, pred[4096]{0:T(1024)(128)(4,1)}, u32[]{:S(2)}) copy-start(pred[4096]{0:T(1024)(128)(4,1)} %constant.245) | copy-start | bytes 12292
  17.0 21.9 %copy-start.6 = (pred[4096]{0:T(1024)(128)(4,1)S(1)}, pred[4096]{0:T(1024)(128)(4,1)}, u32[]{:S(2)}) copy-start(pred[4096]{0:T(1024)(128)(4,1)} %constant.244) | copy-start | bytes 12292
  17.0 21.9 %copy-start.7 = (pred[4096]{0:T(1024)(128)(4,1)S(1)}, pred[4096]{0:T(1024)(128)(4,1)}, u32[]{:S(2)}) copy-start(pred[4096]{0:T(1024)(128)(4,1)} %constant.243) | copy-start | bytes 12292
  17.0 451.3 %all-to-all-start = ((bf16[128,32,256]{2,0,1:T(8,128)(2,1)}), bf16[128,32,256]{2,0,1:T(8,128)(2,1)S(1)}, u32[]{:S(2)}, u32[]{:S(2)}) async-start(bf16[128,32,256]{2,0,1:T(8,128)(2,1)} %copy.21), calls=%async_computation | async-start | bytes 4194304 | tf_op jit(solution)/shard_map/all_to_all | solution.py:122
  33.1 428.1 %all-reduce.2.cloned.1.call-start = ((), (), s32[]{:S(2)}) async-start(), calls=%async_computation.2 | async-start | bytes 2097152 | tf_op jit(solution)/shard_map/psum | solution.py:109
  35.7 727.3 %reduce-scatter.4.cloned.1.call-start = ((), (), s32[]{:S(2)}) async-start(), calls=%async_computation.4 | async-start | bytes 2162688
  484.7 8.9 %copy-start.8 = (s32[64]{0:T(128)S(1)}, s32[64]{0:T(128)}, u32[]{:S(2)}) copy-start(s32[64]{0:T(128)} %param.22) | copy-start | bytes 772
  491.4 27.6 %collective-permute-start = (bf16[4096,256]{1,0:T(8,128)(2,1)}, bf16[4096,256]{1,0:T(8,128)(2,1)S(1)}, u32[]{:S(2)}, u32[]{:S(2)}) collective-permute-start(bf16[4096,256]{1,0:T(8,128)(2,1)} %scatter_fusion), channel_id=1, source_target_pairs={{0,1},{1,2},{2,3},{3,4},{4,5},{5,6},{6,7},{7,8},{8,9},{9,10},{10,1... | collective-permute-start | bytes 6291464 | tf_op jit(solution)/shard_map/ppermute | solution.py:21
  518.9 1.8 copy-start.10
  520.7 5.8 copy-start.2
  520.7 5.8 copy-start.1
Sparse Core Ops, SparseCore 0:
  10.4 132.8 all-gather.1
  146.2 315.0 all-reduce.1
  538.0 224.9 reduce-scatter.3
where the time goes:
time: 772 us; the launch traced here: 771 us
  waiting for transfers between devices  661 us (86%)
  local copies, waits for them, and re-layouts  29.9 us (4%)
  other arithmetic  29 us (4%)
  matrix products  19.2 us (2%)
  starting transfers between devices  18.5 us (2%)
  between operations  13.5 us (2%)
    psum x1, waiting for transfers between devices, local(): lax.psum(pair_term.astype(jnp.bfloat16), 'blk').astype(jnp.float32)  316 us
    unnamed x4, waiting for transfers between devices  225 us
    all_gather x1, waiting for transfers between devices, local(): lax.all_gather(recompute_input, 'blk', axis=1, tiled=True)  102 us
    ppermute x1, waiting for transfers between devices, shifted(): return lax.ppermute(shard, axis, pairs)  18.3 us
    all_to_all x1, starting transfers between devices, local(): lax.all_to_all(jnp.take(cache_entries, targets, axis=1), 'blk', split_axi...  16.1 us
  transfers between devices with their start and end apart: 5, of which 4 were waited for; matrix products, arithmetic and copies ran while one was open for 4% of the time, Pallas kernels for 0%

commit v1 on v0

--- a/solution.py
+++ b/solution.py
@@ -106,7 +106,9 @@
     )
     own_scaled = (recompute_input.astype(jnp.float32) * own_gain[None, :]).astype(jnp.bfloat16)
     pair_term = jnp.dot(own_scaled, w_keyval, preferred_element_type=jnp.float32)
-    pair_sum = lax.psum(pair_term.astype(jnp.bfloat16), "blk").astype(jnp.float32)
+    pair_sum = jnp.sum(lax.all_gather(pair_term.astype(jnp.bfloat16), "blk"), axis=0).astype(
+        jnp.float32
+    )
     inv_rms = lax.rsqrt(square_acc / width + NORM_EPS)
     pair_heads = (pair_sum * inv_rms[:, None]).reshape(slots, KVH, 2 * HEAD_DIM)
     own_pair = lax.dynamic_index_in_dim(pair_heads, own_group, 1, keepdims=False)

time: 772 us -> 830 us (1.075)
  waiting for transfers between devices: 661 us -> 702 us
  other arithmetic: 29 us -> 49.8 us
    all_gather x0 -> x1, waiting for transfers between devices: none -> 380 us  [local(): lax.all_gather(pair_term.astype(jnp.bfloat16), 'blk')]
    psum x1 -> x0, waiting for transfers between devices: 316 us -> none  [local(): lax.psum(pair_term.astype(jnp.bfloat16), 'blk').astype(jnp.float32)]
    all_gather x1, waiting for transfers between devices: 102 us -> 32.2 us  [local(): lax.all_gather(recompute_input, 'blk', axis=1, tiled=True)]
    all_to_all x1, waiting for transfers between devices: 0.01 us -> 47.1 us  [local(): lax.all_to_all(jnp.take(cache_entries, targets, axis=1), 'blk', split_axi...]
    reduce_sum x0 -> x1, other arithmetic: none -> 11.5 us  [local(): jnp.sum(lax.all_gather(pair_term.astype(jnp.bfloat16), 'blk'), axis=0)]
  transfers between devices with their start and end apart: 5 -> 5, of which waited for: 4 -> 5; matrix products, arithmetic and copies ran while one was open for 4% -> 6% of each run, Pallas kernels for 0% -> 0%
where the time goes in v1:
time: 830 us; the launch traced here: 829 us
  waiting for transfers between devices  702 us (85%)
  other arithmetic  49.8 us (6%)
  local copies, waits for them, and re-layouts  26.1 us (3%)
  matrix products  18.7 us (2%)
  starting transfers between devices  18.3 us (2%)
  between operations  13.4 us (2%)
    all_gather x1, waiting for transfers between devices, local(): lax.all_gather(pair_term.astype(jnp.bfloat16), 'blk')  380 us
    unnamed x4, waiting for transfers between devices  226 us
    all_to_all x1, waiting for transfers between devices, local(): lax.all_to_all(jnp.take(cache_entries, targets, axis=1), 'blk', split_axi...  47.1 us
    all_gather x1, waiting for transfers between devices, local(): lax.all_gather(recompute_input, 'blk', axis=1, tiled=True)  32.2 us
    ppermute x1, waiting for transfers between devices, shifted(): return lax.ppermute(shard, axis, pairs)  16.9 us
  transfers between devices with their start and end apart: 5, of which 5 were waited for; matrix products, arithmetic and copies ran while one was open for 6% of the time, Pallas kernels for 0%

profile of v1, /device:TPU:2, one launch (start us, length us, event | category | flops | bytes accessed | tf_op | source)
XLA Modules:
  0.0 828.7 jit_solution(376086353432289511)
XLA Ops:
  8.1 2.5 convolution_convert_fusion.1
  11.3 7.8 gather_fusion
  19.1 4.2 copy.23
  23.3 16.0 %all-to-all-start = ((bf16[128,32,256]{2,0,1:T(8,128)(2,1)}), bf16[128,32,256]{2,0,1:T(8,128)(2,1)S(1)}, u32[]{:S(2)}, u32[]{:S(2)}) async-start(bf16[128,32,256]{2,0,1:T(8,128)(2,1)} %copy.23), calls=%async_computation | async-start | bytes 4194304 | tf_op jit(solution)/shard_map/all_to_all | solution.py:124
  40.2 2.0 and_select_fusion
  43.1 2.6 select_convert_fusion.1
  45.7 47.1 %all-to-all-done = bf16[128,32,256]{2,0,1:T(8,128)(2,1)S(1)} async-done(((bf16[128,32,256]{2,0,1:T(8,128)(2,1)}), bf16[128,32,256]{2,0,1:T(8,128)(2,1)S(1)}, u32[]{:S(2)}, u32[]{:S(2)}) %all-to-all-start) | async-done | bytes 2097184 | tf_op jit(solution)/shard_map/all_to_all | solution.py:124
  96.0 5.3 fusion.57
  103.3 3.6 pad_maximum_fusion
  106.9 2.3 gather_fusion.1
  109.2 32.2 %all-gather.4.cloned.1.call-done = bf16[256,4096]{1,0:T(8,128)(2,1)} async-done(((bf16[256,128]{1,0:T(8,128)(2,1)}), bf16[256,4096]{1,0:T(8,128)(2,1)}) %all-gather.4.cloned.1.call-update) | async-done | bytes 2097168 | tf_op jit(solution)/shard_map/all_gather | solution.py:99
  141.4 2.1 fusion.4
  145.4 380.2 %all-gather.6.cloned.1.call-done = bf16[8192,2048]{1,0:T(8,128)(2,1)} async-done(((bf16[256,2048]{1,0:T(8,128)(2,1)}), bf16[8192,2048]{1,0:T(8,128)(2,1)}) %all-gather.6.cloned.1.call-update) | async-done | bytes 33554448 | tf_op jit(solution)/shard_map/all_gather | solution.py:109
  525.6 11.5 %reduce_sum.68 = bf16[256,2048]{1,0:T(8,128)(2,1)S(1)} reduce(bf16[32,256,2048]{2,1,0:T(8,128)(2,1)} %bitcast.67, bf16[]{:T(256)} %constant.220.clone.1), dimensions={0}, to_apply=%region_2.3 | reduce | flops 16252928 | bytes 34603008 | tf_op jit(solution)/shard_map/reduce_sum | solution.py:109
  543.0 5.1 scatter_custom_fusion
  548.1 2.1 collective-permute-start
  552.8 2.0 fusion.36
  555.2 3.5 fusion.115
  558.8 16.9 %collective-permute-done = bf16[4096,256]{1,0:T(8,128)(2,1)S(1)} collective-permute-done((bf16[4096,256]{1,0:T(8,128)(2,1)}, bf16[4096,256]{1,0:T(8,128)(2,1)S(1)}, u32[]{:S(2)}, u32[]{:S(2)}) %collective-permute-start) | collective-permute-done | bytes 2097184 | tf_op jit(solution)/shard_map/ppermute | solution.py:21
  577.4 5.8 fusion.12
  583.3 3.0 fusion.39
  586.3 5.8 convolution_convert_fusion
  592.1 2.5 copy.35
  595.2 225.2 %reduce-scatter.4.cloned.1.call-done = bf16[128,256]{1,0:T(8,128)(2,1)} async-done(((bf16[4096,256]{1,0:T(8,128)(2,1)}), bf16[128,256]{1,0:T(8,128)(2,1)}) %reduce-scatter.4.cloned.1.call-update) | async-done | bytes 65552
  (68 shorter events, 24.0 us)
Async XLA Ops:
  6.5 579.8 %copy-start = (bf16[128,4096]{1,0:T(8,128)(2,1)S(1)}, bf16[128,4096]{1,0:T(8,128)(2,1)}, u32[]{:S(2)}) copy-start(bf16[128,4096]{1,0:T(8,128)(2,1)} %param.19) | copy-start | bytes 3145732
  6.5 4.7 copy-start.1
  6.5 134.9 %all-gather.4.cloned.1.call-start = ((), (), s32[]{:S(2)}) async-start(), calls=%async_computation.2 | async-start | bytes 2162688 | tf_op jit(solution)/shard_map/all_gather | solution.py:99
  7.3 518.3 %all-gather.6.cloned.1.call-start = ((), (), s32[]{:S(2)}) async-start(), calls=%async_computation.3 | async-start | bytes 34603008 | tf_op jit(solution)/shard_map/all_gather | solution.py:109
  19.1 20.5 %copy-start.10 = (s32[16]{0:T(128)S(1)}, s32[16]{0:T(128)}, u32[]{:S(2)}) copy-start(s32[16]{0:T(128)} %param.24) | copy-start | bytes 196
  19.1 23.0 %copy-start.11 = (s32[64]{0:T(128)S(1)}, s32[64]{0:T(128)}, u32[]{:S(2)}) copy-start(s32[64]{0:T(128)} %param.20) | copy-start | bytes 772
  19.1 23.1 %copy-start.8 = (s32[64]{0:T(128)S(1)}, s32[64]{0:T(128)}, u32[]{:S(2)}) copy-start(s32[64]{0:T(128)} %param.21) | copy-start | bytes 772
  19.1 24.0 %copy-start.5 = (pred[4096]{0:T(1024)(128)(4,1)S(1)}, pred[4096]{0:T(1024)(128)(4,1)}, u32[]{:S(2)}) copy-start(pred[4096]{0:T(1024)(128)(4,1)} %constant.247) | copy-start | bytes 12292
  19.1 24.0 %copy-start.6 = (pred[4096]{0:T(1024)(128)(4,1)S(1)}, pred[4096]{0:T(1024)(128)(4,1)}, u32[]{:S(2)}) copy-start(pred[4096]{0:T(1024)(128)(4,1)} %constant.246) | copy-start | bytes 12292
  19.1 23.9 %copy-start.7 = (pred[4096]{0:T(1024)(128)(4,1)S(1)}, pred[4096]{0:T(1024)(128)(4,1)}, u32[]{:S(2)}) copy-start(pred[4096]{0:T(1024)(128)(4,1)} %constant.245) | copy-start | bytes 12292
  23.3 69.5 %all-to-all-start = ((bf16[128,32,256]{2,0,1:T(8,128)(2,1)}), bf16[128,32,256]{2,0,1:T(8,128)(2,1)S(1)}, u32[]{:S(2)}, u32[]{:S(2)}) async-start(bf16[128,32,256]{2,0,1:T(8,128)(2,1)} %copy.23), calls=%async_computation | async-start | bytes 4194304 | tf_op jit(solution)/shard_map/all_to_all | solution.py:124
  39.3 781.2 %reduce-scatter.4.cloned.1.call-start = ((), (), s32[]{:S(2)}) async-start(), calls=%async_computation.4 | async-start | bytes 2162688
  538.7 14.2 %copy-start.4 = (bf16[256,4096]{1,0:T(8,128)(2,1)S(1)}, bf16[256,4096]{1,0:T(8,128)(2,1)}, u32[]{:S(2)}) copy-start(bf16[256,4096]{1,0:T(8,128)(2,1)} %all-gather.4.cloned.1.call-done) | copy-start | bytes 6291460
  548.1 27.6 %collective-permute-start = (bf16[4096,256]{1,0:T(8,128)(2,1)}, bf16[4096,256]{1,0:T(8,128)(2,1)S(1)}, u32[]{:S(2)}, u32[]{:S(2)}) collective-permute-start(bf16[4096,256]{1,0:T(8,128)(2,1)} %scatter_custom_fusion), channel_id=1, source_target_pairs={{0,1},{1,2},{2,3},{3,4},{4,5},{5,6},{6,7},{7,8},{8,9},{9,10},{10,1... | collective-permute-start | bytes 6291464 | tf_op jit(solution)/shard_map/ppermute | solution.py:21
  575.6 1.8 copy-start.9
  577.4 5.8 copy-start.2
  577.4 5.8 copy-start.3
Sparse Core Ops, SparseCore 0:
  10.4 130.9 all-gather.3
  144.6 380.9 all-gather.5
  594.7 225.7 reduce-scatter.3
